TPU v7x, 32 devices: a whole 2x2x4 slice. The times are simulated.
32 devices in a mesh: pipe: 8 (over z, y), tensor: 4 (over x, core).
Axes of the slice: x: 2, y: 2, z: 4, core: 2. Of those that a mesh axis runs over, the one named last changes fastest.
Arguments:
- arriving: float32 [8, 8192, 384], P('pipe', 'tensor'), may hold values from -6 to 6
- stash: bfloat16 [2, 8, 8192, 384], P(None, 'pipe', 'tensor'), may hold values from -6 to 6
- grad_in: float32 [8, 8192, 384], P('pipe', 'tensor'), may hold values from -6 to 6
- first_up: bfloat16 [8, 64, 128, 128], P('pipe', 'tensor'), may hold values from -0.5 to 0.5
- second_up: bfloat16 [8, 128, 64, 256], P('pipe', 'tensor'), may hold values from -0.75 to 0.75
- first_down: bfloat16 [8, 128, 64, 256], P('pipe', 'tensor'), may hold values from -0.375 to 0.375
- second_down: bfloat16 [8, 64, 128, 128], P('pipe', 'tensor'), may hold values from -0.5 to 0.5
Outputs:
- arriving_out: float32 [8, 8192, 384], P('pipe', 'tensor')
- grad_out: float32 [8, 8192, 384], P('pipe', 'tensor')
- first_up_grad: float32 [8, 64, 128, 128], P('pipe', 'tensor')
- second_up_grad: float32 [8, 128, 64, 256], P('pipe', 'tensor')
- first_down_grad: float32 [8, 128, 64, 256], P('pipe', 'tensor')
- second_down_grad: float32 [8, 64, 128, 128], P('pipe', 'tensor')
All inputs are finite; a program needn't handle non-finite values.
Results may differ from a plain program's by a relative error of at most 0.007.
Values may be sent and summed in bfloat16 or wider, within the bound.
No kernel may reach another device: no remote copies, remote signals or barrier semaphores. Data moves between devices by JAX's collectives and lax.ppermute only.
A program may use at most 192 MiB of HBM per device.

v0:
```python
import jax
import jax.numpy as jnp
from jax import lax
from jax.sharding import PartitionSpec as P


def shifted(value, axis, by):
    count = lax.axis_size(axis)
    return lax.ppermute(value, axis, [(i, (i + by) % count) for i in range(count)])


def smooth(values):
    return jax.nn.gelu(values, approximate=True)


def to_columns(value):
    return lax.all_to_all(value, "tensor", split_axis=1, concat_axis=0, tiled=True)


def to_rows(value):
    return lax.all_to_all(value, "tensor", split_axis=0, concat_axis=1, tiled=True)


def front(narrow_in, first_up, second_up, first_down):
    first_out = jnp.einsum(
        "njr,nji->nir", narrow_in, first_up, preferred_element_type=jnp.float32
    ).astype(jnp.bfloat16)
    spread = to_columns(first_out)
    hidden_pre = jnp.einsum("nir,inf->ifr", spread, second_up, preferred_element_type=jnp.float32)
    hidden = smooth(hidden_pre).astype(jnp.bfloat16)
    local_fold = jnp.einsum(
        "ifr,inf->nir", hidden, first_down, preferred_element_type=jnp.float32
    ).astype(jnp.bfloat16)
    folded = to_rows(local_fold)
    return (spread, hidden_pre, hidden, folded)


def backward(narrow_in, cotangent, first_up, second_up, first_down, second_down, parts):
    spread, hidden_pre, hidden, folded = parts
    narrow_grad = cotangent.astype(jnp.bfloat16).reshape(narrow_in.shape)
    grad_second_down = jnp.einsum(
        "nir,nkr->nik", folded, narrow_grad, preferred_element_type=jnp.float32
    )
    local_grad = jnp.einsum(
        "nkr,nik->nir", narrow_grad, second_down, preferred_element_type=jnp.float32
    ).astype(jnp.bfloat16)
    grad_folded = to_columns(local_grad)
    grad_first_down = jnp.einsum(
        "ifr,nir->inf", hidden, grad_folded, preferred_element_type=jnp.float32
    )
    grad_hidden = jnp.einsum(
        "nir,inf->ifr", grad_folded, first_down, preferred_element_type=jnp.float32
    )
    smooth_back = jax.vjp(smooth, hidden_pre)[1]
    grad_pre = smooth_back(grad_hidden)[0].astype(jnp.bfloat16)
    grad_second_up = jnp.einsum(
        "nir,ifr->inf", spread, grad_pre, preferred_element_type=jnp.float32
    )
    column_grad = jnp.einsum(
        "ifr,inf->nir", grad_pre, second_up, preferred_element_type=jnp.float32
    ).astype(jnp.bfloat16)
    grad_first = to_rows(column_grad)
    grad_first_up = jnp.einsum(
        "njr,nir->nji", narrow_in, grad_first, preferred_element_type=jnp.float32
    )
    grad_input = jnp.einsum(
        "nir,nji->njr", grad_first, first_up, preferred_element_type=jnp.float32
    ).reshape(cotangent.shape)
    return (grad_input, (grad_first_up, grad_second_up, grad_first_down, grad_second_down))


def body(arriving, stash, grad_in, first_up, second_up, first_down, second_down):
    activation = arriving[0]
    cotangent = grad_in[0]
    up_first = first_up[0]
    up_second = second_up[0]
    down_first = first_down[0]
    down_second = second_down[0]
    blocks = up_first.shape[0]
    width = up_first.shape[1]
    rows = activation.shape[1]
    far_activation = shifted(activation, "pipe", 2)
    far_cotangent = shifted(cotangent, "pipe", -2)
    current = activation.astype(jnp.bfloat16).reshape(blocks, width, rows)
    folded_ahead = front(current, up_first, up_second, down_first)[3]
    step = jnp.einsum(
        "nir,nik->nkr", folded_ahead, down_second, preferred_element_type=jnp.float32
    ).reshape(activation.shape)
    output = activation + step
    near_activation = shifted(output.astype(jnp.bfloat16), "pipe", 1)
    step, cotangent = lax.optimization_barrier((step, cotangent))
    stored = stash[0, 0].reshape(blocks, width, rows)
    behind = front(stored, up_first, up_second, down_first)
    grad_step, totals = backward(
        stored, cotangent, up_first, up_second, down_first, down_second, behind
    )
    grad_input = cotangent + grad_step
    near_cotangent = shifted(grad_input.astype(jnp.bfloat16), "pipe", -1)
    step, grad_step, far_activation, far_cotangent = lax.optimization_barrier(
        (step, grad_step, far_activation, far_cotangent)
    )
    far_step = shifted(step.astype(jnp.bfloat16), "pipe", 2)
    far_grad_step = shifted(grad_step.astype(jnp.bfloat16), "pipe", -2)
    current = near_activation.reshape(blocks, width, rows)
    folded_ahead = front(current, up_first, up_second, down_first)[3]
    step = jnp.einsum(
        "nir,nik->nkr", folded_ahead, down_second, preferred_element_type=jnp.float32
    ).reshape(activation.shape)
    last_step = shifted(step.astype(jnp.bfloat16), "pipe", 1)
    step, near_cotangent, far_step, far_grad_step = lax.optimization_barrier(
        (step, near_cotangent, far_step, far_grad_step)
    )
    stored = stash[1, 0].reshape(blocks, width, rows)
    behind = front(stored, up_first, up_second, down_first)
    grad_step, terms = backward(
        stored, near_cotangent, up_first, up_second, down_first, down_second, behind
    )
    last_grad_step = shifted(grad_step.astype(jnp.bfloat16), "pipe", -1)
    activation = far_activation + (far_step.astype(jnp.float32) + last_step.astype(jnp.float32))
    cotangent = far_cotangent + (
        far_grad_step.astype(jnp.float32) + last_grad_step.astype(jnp.float32)
    )
    totals = (
        totals[0] + terms[0],
        totals[1] + terms[1],
        totals[2] + terms[2],
        totals[3] + terms[3],
    )
    return (
        activation[None],
        cotangent[None],
        totals[0][None],
        totals[1][None],
        totals[2][None],
        totals[3][None],
    )


def solution(mesh):
    placed = (
        P("pipe", "tensor", None),
        P(None, "pipe", "tensor", None),
        P("pipe", "tensor", None),
        P("pipe", "tensor", None, None),
        P("pipe", "tensor", None, None),
        P("pipe", "tensor", None, None),
        P("pipe", "tensor", None, None),
    )
    return jax.shard_map(
        body,
        mesh=mesh,
        in_specs=placed,
        out_specs=(
            P("pipe", "tensor", None),
            P("pipe", "tensor", None),
            P("pipe", "tensor", None, None),
            P("pipe", "tensor", None, None),
            P("pipe", "tensor", None, None),
            P("pipe", "tensor", None, None),
        ),
        check_vma=False,
    )
```

profile of v0, /device:TPU:0, one launch (start us, length us, event | category | flops | bytes accessed | tf_op | source)
XLA Modules:
  0.0 497.8 jit_solution(13819847129199727905)
XLA Ops:
  16.0 14.7 %all-to-all-done = bf16[16,128,384]{2,0,1:T(8,128)(2,1)} async-done(((bf16[16,128,384]{2,0,1:T(8,128)(2,1)}), bf16[16,128,384]{2,0,1:T(8,128)(2,1)}, u32[]{:S(2)}, u32[]{:S(2)}) %all-to-all-start) | async-done | bytes 1572896 | tf_op jit(solution)/shard_map/all_to_all | solution.py:17
  37.8 7.6 %fusion.55 = bf16[64,32,384]{2,0,1:T(8,128)(2,1)} fusion(bf16[64,32,384]{2,0,1:T(8,128)(2,1)} %bitcast.292, bf16[1,32,64,256]{3,2,1,0:T(8,128)(2,1)} %param.12, bf16[1,32,64,256]{3,2,1,0:T(8,128)(2,1)S(1)} %copy-done), kind=kOutput, calls=%fused_computation.74 | convolution fusion | flops 834404352 | bytes 5242880 | tf_op jit(solution)/shard_map/ifr,inf->nir/dot_general | solution.py:31
  48.9 6.2 %all-to-all-done.8 = bf16[16,128,384]{2,0,1:T(8,128)(2,1)} async-done(((bf16[16,128,384]{2,0,1:T(8,128)(2,1)}), bf16[16,128,384]{2,0,1:T(8,128)(2,1)}, u32[]{:S(2)}, u32[]{:S(2)}) %all-to-all-start.8) | async-done | bytes 1572896 | tf_op jit(solution)/shard_map/all_to_all | solution.py:17
  55.1 4.4 all-to-all-start.1
  62.2 17.4 %all-to-all-done.1 = bf16[64,32,384]{2,1,0:T(8,128)(2,1)} async-done(((bf16[64,32,384]{2,1,0:T(8,128)(2,1)}), bf16[64,32,384]{2,1,0:T(8,128)(2,1)}, u32[]{:S(2)}, u32[]{:S(2)}) %all-to-all-start.1) | async-done | bytes 1572896 | tf_op jit(solution)/shard_map/all_to_all | solution.py:21
  79.7 4.5 all-to-all-start.3
  84.2 4.5 collective-permute-start.1
  108.7 6.4 %fusion.74 = f32[32,384,256]{2,1,0:T(8,128)} fusion(bf16[64,32,384]{2,0,1:T(8,128)(2,1)S(1)} %bitcast.273, bf16[1,32,64,256]{3,2,1,0:T(8,128)(2,1)S(1)} %copy-done), kind=kOutput, calls=%fused_computation.93 | convolution fusion | flops 402653184 | bytes 15204352 | tf_op jit(solution)/shard_map/nir,inf->ifr/dot_general | solution.py:29
  118.0 8.6 %fusion.34 = (bf16[32,256,384]{1,2,0:T(8,128)(2,1)}, f32[32,384,256]{2,1,0:T(8,128)}) fusion(bf16[64,32,384]{2,0,1:T(8,128)(2,1)S(1)} %bitcast.281, bf16[1,32,64,256]{3,2,1,0:T(8,128)(2,1)S(1)} %copy-done), kind=kOutput, calls=%fused_computation.45 | convolution fusion | flops 430964736 | bytes 21495808 | tf_op jit(solution)/shard_map/nir,inf->ifr/dot_general | solution.py:29
  130.6 12.2 %fusion.6 = bf16[32,256,384]{1,2,0:T(8,128)(2,1)S(1)} fusion(f32[32,384,256]{2,1,0:T(8,128)} %get-tuple-element.45, bf16[64,32,384]{2,0,1:T(8,128)(2,1)S(1)} %bitcast.283, bf16[1,32,64,256]{3,2,1,0:T(8,128)(2,1)S(1)} %copy-done.28), kind=kOutput, calls=%fused_computation.12 | convolution fusion | flops 465567744 | bytes 21495808 | tf_op jit(solution)/shard_map/nir,inf->ifr/dot_general | solution.py:51
  147.4 4.6 all-to-all-start.4
  152.0 7.9 %fusion.61 = bf16[64,32,384]{2,0,1:T(8,128)(2,1)S(1)} fusion(bf16[1,32,64,256]{3,2,1,0:T(8,128)(2,1)S(1)} %copy-done.28, f32[32,384,256]{2,1,0:T(8,128)} %fusion.74), kind=kOutput, calls=%fused_computation.78 | convolution fusion | flops 431751168 | bytes 15204352 | tf_op jit(solution)/shard_map/ifr,inf->nir/dot_general | solution.py:31
  162.0 10.1 %all-to-all-done.4 = bf16[64,32,384]{2,1,0:T(8,128)(2,1)} async-done(((bf16[64,32,384]{2,1,0:T(8,128)(2,1)}), bf16[64,32,384]{2,1,0:T(8,128)(2,1)}, u32[]{:S(2)}, u32[]{:S(2)}) %all-to-all-start.4) | async-done | bytes 1572896 | tf_op jit(solution)/shard_map/all_to_all | solution.py:21
  176.5 4.4 add_convert_fusion.1
  189.8 35.5 %collective-permute-done = f32[2048,384]{1,0:T(8,128)} collective-permute-done((f32[2048,384]{1,0:T(8,128)}, f32[2048,384]{1,0:T(8,128)}, u32[]{:S(2)}, u32[]{:S(2)}) %collective-permute-start) | collective-permute-done | bytes 3145760 | tf_op jit(solution)/shard_map/ppermute | solution.py:9
  228.0 4.4 all-to-all-start.10
  242.2 18.3 %collective-permute-done.2 = bf16[2048,384]{1,0:T(8,128)(2,1)} collective-permute-done((bf16[2048,384]{1,0:T(8,128)(2,1)}, bf16[2048,384]{1,0:T(8,128)(2,1)}, u32[]{:S(2)}, u32[]{:S(2)}) %collective-permute-start.2) | collective-permute-done | bytes 1572896 | tf_op jit(solution)/shard_map/ppermute | solution.py:9
  266.6 4.4 all-to-all-start.5
  277.4 16.2 %collective-permute-done.3 = bf16[2048,384]{1,0:T(8,128)(2,1)} collective-permute-done((bf16[2048,384]{1,0:T(8,128)(2,1)}, bf16[2048,384]{1,0:T(8,128)(2,1)}, u32[]{:S(2)}, u32[]{:S(2)}) %collective-permute-start.3) | collective-permute-done | bytes 1572896 | tf_op jit(solution)/shard_map/ppermute | solution.py:9
  293.7 15.2 %collective-permute-done.5 = bf16[2048,384]{1,0:T(8,128)(2,1)} collective-permute-done((bf16[2048,384]{1,0:T(8,128)(2,1)}, bf16[2048,384]{1,0:T(8,128)(2,1)}, u32[]{:S(2)}, u32[]{:S(2)}) %collective-permute-start.5) | collective-permute-done | bytes 1572896 | tf_op jit(solution)/shard_map/ppermute | solution.py:9
  308.9 34.2 %collective-permute-done.4 = bf16[2048,384]{1,0:T(8,128)(2,1)} collective-permute-done((bf16[2048,384]{1,0:T(8,128)(2,1)}, bf16[2048,384]{1,0:T(8,128)(2,1)}, u32[]{:S(2)}, u32[]{:S(2)}) %collective-permute-start.4) | collective-permute-done | bytes 1572896 | tf_op jit(solution)/shard_map/ppermute | solution.py:9
  349.2 4.8 all-to-all-start.7
  354.0 5.8 %fusion.109 = f32[32,64,256]{2,1,0:T(8,128)} fusion(bf16[64,32,384]{2,0,1:T(8,128)(2,1)} %bitcast.284, bf16[32,256,384]{1,2,0:T(8,128)(2,1)} %get-tuple-element.44), kind=kOutput, calls=%fused_computation.125 | convolution fusion | flops 402653184 | bytes 9961472 | tf_op jit(solution)/shard_map/ifr,nir->inf/dot_general | solution.py:48
  362.7 7.6 %fusion.52 = bf16[64,32,384]{2,0,1:T(8,128)(2,1)} fusion(bf16[64,32,384]{2,0,1:T(8,128)(2,1)} %bitcast.293, bf16[1,32,64,256]{3,2,1,0:T(8,128)(2,1)} %param.12, bf16[1,32,64,256]{3,2,1,0:T(8,128)(2,1)S(1)} %copy-done), kind=kOutput, calls=%fused_computation.73 | convolution fusion | flops 834404352 | bytes 5242880 | tf_op jit(solution)/shard_map/ifr,inf->nir/dot_general | solution.py:31
  374.1 4.5 all-to-all-start.6
  380.5 12.2 %fusion.13 = bf16[32,256,384]{1,2,0:T(8,128)(2,1)S(1)} fusion(f32[32,384,256]{2,1,0:T(8,128)} %fusion.74, bf16[64,32,384]{2,0,1:T(8,128)(2,1)S(1)} %bitcast.290, bf16[1,32,64,256]{3,2,1,0:T(8,128)(2,1)S(1)} %copy-done.30), kind=kOutput, calls=%fused_computation.19 | convolution fusion | flops 465567744 | bytes 21495808 | tf_op jit(solution)/shard_map/nir,inf->ifr/dot_general | solution.py:51
  403.2 5.9 %fusion.108 = f32[32,64,256]{2,1,0:T(8,128)} fusion(bf16[64,32,384]{2,0,1:T(8,128)(2,1)} %bitcast.282, bf16[32,256,384]{1,2,0:T(8,128)(2,1)} %copy-done.3), kind=kOutput, calls=%fused_computation.124 | convolution fusion | flops 402653184 | bytes 9961472 | tf_op jit(solution)/shard_map/nir,ifr->inf/dot_general | solution.py:56
  417.6 5.7 %all-to-all-done.9 = bf16[64,32,384]{2,1,0:T(8,128)(2,1)} async-done(((bf16[64,32,384]{2,1,0:T(8,128)(2,1)}), bf16[64,32,384]{2,1,0:T(8,128)(2,1)}, u32[]{:S(2)}, u32[]{:S(2)}) %all-to-all-start.9) | async-done | bytes 1572896 | tf_op jit(solution)/shard_map/all_to_all | solution.py:21
  427.1 9.5 %add_bitcast_fusion.2 = f32[1,32,64,256]{3,2,1,0:T(8,128)} fusion(f32[32,64,256]{2,1,0:T(8,128)S(1)} %copy-done.25, bf16[64,32,384]{2,0,1:T(8,128)(2,1)S(1)} %bitcast.291, f32[32,384,256]{2,1,0:T(8,128)} %fusion.74), kind=kOutput, calls=%fused_computation.58 | convolution fusion | flops 431489024 | bytes 18350080 | tf_op jit(solution)/shard_map/ifr,nir->inf/dot_general | solution.py:48
  439.2 47.0 %collective-permute-done.6 = bf16[2048,384]{1,0:T(8,128)(2,1)S(1)} collective-permute-done((bf16[2048,384]{1,0:T(8,128)(2,1)}, bf16[2048,384]{1,0:T(8,128)(2,1)S(1)}, u32[]{:S(2)}, u32[]{:S(2)}) %collective-permute-start.6) | collective-permute-done | bytes 1572896 | tf_op jit(solution)/shard_map/ppermute | solution.py:9
  486.1 4.4 add_bitcast_fusion.1
  492.7 4.9 add_bitcast_fusion
  (142 shorter events, 142.0 us)
Async XLA Ops:
  0.6 37.2 %copy-start = (bf16[1,32,64,256]{3,2,1,0:T(8,128)(2,1)S(1)}, bf16[1,32,64,256]{3,2,1,0:T(8,128)(2,1)}, u32[]{:S(2)}) copy-start(bf16[1,32,64,256]{3,2,1,0:T(8,128)(2,1)} %param.11) | copy-start | bytes 3145732
  5.5 25.1 %all-to-all-start = ((bf16[16,128,384]{2,0,1:T(8,128)(2,1)}), bf16[16,128,384]{2,0,1:T(8,128)(2,1)}, u32[]{:S(2)}, u32[]{:S(2)}) async-start(bf16[16,128,384]{2,0,1:T(8,128)(2,1)} %copy.78), calls=%async_computation | async-start | bytes 3145728 | tf_op jit(solution)/shard_map/all_to_all | solution.py:17
  12.1 47.4 %copy-start.9 = (bf16[1,1,2048,384]{3,2,1,0:T(8,128)(2,1)}, bf16[1,1,2048,384]{3,2,1,0:T(8,128)(2,1)S(1)}, u32[]{:S(2)}) copy-start(bf16[1,1,2048,384]{3,2,1,0:T(8,128)(2,1)S(1)} %get-tuple-element.43) | copy-start | bytes 4718596
  30.6 24.5 %all-to-all-start.8 = ((bf16[16,128,384]{2,0,1:T(8,128)(2,1)}), bf16[16,128,384]{2,0,1:T(8,128)(2,1)}, u32[]{:S(2)}, u32[]{:S(2)}) async-start(bf16[16,128,384]{2,0,1:T(8,128)(2,1)} %copy.107), calls=%async_computation.8 | async-start | bytes 3145728 | tf_op jit(solution)/shard_map/all_to_all | solution.py:17
  55.1 24.5 %all-to-all-start.1 = ((bf16[64,32,384]{2,1,0:T(8,128)(2,1)}), bf16[64,32,384]{2,1,0:T(8,128)(2,1)}, u32[]{:S(2)}, u32[]{:S(2)}) async-start(bf16[64,32,384]{2,1,0:T(8,128)(2,1)} %copy.81), calls=%async_computation.1 | async-start | bytes 3145728 | tf_op jit(solution)/shard_map/all_to_all | solution.py:21
  79.7 24.7 %all-to-all-start.3 = ((bf16[16,128,384]{2,0,1:T(8,128)(2,1)}), bf16[16,128,384]{2,0,1:T(8,128)(2,1)}, u32[]{:S(2)}, u32[]{:S(2)}) async-start(bf16[16,128,384]{2,0,1:T(8,128)(2,1)} %copy.89), calls=%async_computation.3 | async-start | bytes 3145728 | tf_op jit(solution)/shard_map/all_to_all | solution.py:17
  84.2 105.6 %collective-permute-start.1 = (f32[2048,384]{1,0:T(8,128)}, f32[2048,384]{1,0:T(8,128)}, u32[]{:S(2)}, u32[]{:S(2)}) collective-permute-start(f32[2048,384]{1,0:T(8,128)} %bitcast.278), channel_id=1, source_target_pairs={{0,24},{4,28},{8,0},{12,4},{16,8},{20,12},{24,16},{28,20},{1,25},{... | collective-permute-start | bytes 9437192 | tf_op jit(solution)/shard_map/ppermute | solution.py:9
  88.7 136.6 %collective-permute-start = (f32[2048,384]{1,0:T(8,128)}, f32[2048,384]{1,0:T(8,128)}, u32[]{:S(2)}, u32[]{:S(2)}) collective-permute-start(f32[2048,384]{1,0:T(8,128)} %bitcast.277), channel_id=1, source_target_pairs={{0,8},{4,12},{8,16},{12,20},{16,24},{20,28},{24,0},{28,4},{1,9},{5... | collective-permute-start | bytes 9437192 | tf_op jit(solution)/shard_map/ppermute | solution.py:9
  90.5 18.2 %copy-start.13 = (bf16[16,4,32,384]{3,0,1,2:T(8,128)(2,1)}, bf16[16,4,32,384]{3,0,1,2:T(8,128)(2,1)S(1)}, u32[]{:S(2)}) copy-start(bf16[16,4,32,384]{3,0,1,2:T(8,128)(2,1)S(1)} %copy.108) | copy-start | bytes 4718596
  104.4 24.5 %all-to-all-start.2 = ((bf16[16,128,384]{2,0,1:T(8,128)(2,1)}), bf16[16,128,384]{2,0,1:T(8,128)(2,1)}, u32[]{:S(2)}, u32[]{:S(2)}) async-start(bf16[16,128,384]{2,0,1:T(8,128)(2,1)} %copy.85), calls=%async_computation.2 | async-start | bytes 3145728 | tf_op jit(solution)/shard_map/all_to_all | solution.py:17
  130.5 12.2 %copy-start.21 = (bf16[4,16,32,384]{3,1,0,2:T(8,128)(2,1)}, bf16[4,16,32,384]{3,1,0,2:T(8,128)(2,1)S(1)}, u32[]{:S(2)}) copy-start(bf16[4,16,32,384]{3,1,0,2:T(8,128)(2,1)S(1)} %copy.87) | copy-start | bytes 4718596
  147.4 24.7 %all-to-all-start.4 = ((bf16[64,32,384]{2,1,0:T(8,128)(2,1)}), bf16[64,32,384]{2,1,0:T(8,128)(2,1)}, u32[]{:S(2)}, u32[]{:S(2)}) async-start(bf16[64,32,384]{2,1,0:T(8,128)(2,1)} %copy.92), calls=%async_computation.4 | async-start | bytes 3145728 | tf_op jit(solution)/shard_map/all_to_all | solution.py:21
  160.0 23.4 %slice-start = ((s8[6291456]{0:T(1024)(128)(4,1)}), s8[2097152]{0:T(1024)(128)(4,1)S(1)}, s32[]{:S(2)}) async-start(s8[6291456]{0:T(1024)(128)(4,1)} %bitcast.261), calls=%async_computation.12 | async-start | bytes 4194304
  172.1 55.8 %all-to-all-start.11 = ((bf16[64,32,384]{2,1,0:T(8,128)(2,1)}), bf16[64,32,384]{2,1,0:T(8,128)(2,1)}, u32[]{:S(2)}, u32[]{:S(2)}) async-start(bf16[64,32,384]{2,1,0:T(8,128)(2,1)} %copy.120), calls=%async_computation.11 | async-start | bytes 3145728 | tf_op jit(solution)/shard_map/all_to_all | solution.py:21
  180.9 79.5 %collective-permute-start.2 = (bf16[2048,384]{1,0:T(8,128)(2,1)}, bf16[2048,384]{1,0:T(8,128)(2,1)}, u32[]{:S(2)}, u32[]{:S(2)}) collective-permute-start(bf16[2048,384]{1,0:T(8,128)(2,1)} %add_convert_fusion.1), channel_id=1, source_target_pairs={{0,4},{4,8},{8,12},{12,16},{16,20},{20,24},{24,28},{28,0},{1,5},{5... | collective-permute-start | bytes 4718600 | tf_op jit(solution)/shard_map/ppermute | solution.py:9
  189.2 36.1 %copy-start.1 = (f32[16,384,128]{1,2,0:T(8,128)S(1)}, f32[16,384,128]{1,2,0:T(8,128)}, u32[]{:S(2)}) copy-start(f32[16,384,128]{1,2,0:T(8,128)} %fusion.87) | copy-start | bytes 9437188
  189.8 36.9 %copy-start.2 = (f32[16,384,128]{1,2,0:T(8,128)}, f32[16,384,128]{1,2,0:T(8,128)S(1)}, u32[]{:S(2)}) copy-start(f32[16,384,128]{1,2,0:T(8,128)S(1)} %fusion.89) | copy-start | bytes 9437188
  228.0 38.6 %all-to-all-start.10 = ((bf16[64,32,384]{2,1,0:T(8,128)(2,1)}), bf16[64,32,384]{2,1,0:T(8,128)(2,1)}, u32[]{:S(2)}, u32[]{:S(2)}) async-start(bf16[64,32,384]{2,1,0:T(8,128)(2,1)} %copy.117), calls=%async_computation.10 | async-start | bytes 3145728 | tf_op jit(solution)/shard_map/all_to_all | solution.py:21
  236.6 57.1 %collective-permute-start.3 = (bf16[2048,384]{1,0:T(8,128)(2,1)}, bf16[2048,384]{1,0:T(8,128)(2,1)}, u32[]{:S(2)}, u32[]{:S(2)}) collective-permute-start(bf16[2048,384]{1,0:T(8,128)(2,1)} %add_convert_fusion), channel_id=1, source_target_pairs={{0,28},{4,0},{8,4},{12,8},{16,12},{20,16},{24,20},{28,24},{1,29},{... | collective-permute-start | bytes 4718600 | tf_op jit(solution)/shard_map/ppermute | solution.py:9
  240.1 68.8 %collective-permute-start.5 = (bf16[2048,384]{1,0:T(8,128)(2,1)}, bf16[2048,384]{1,0:T(8,128)(2,1)}, u32[]{:S(2)}, u32[]{:S(2)}) collective-permute-start(bf16[2048,384]{1,0:T(8,128)(2,1)} %convert_element_type.148), channel_id=1, source_target_pairs={{0,24},{4,28},{8,0},{12,4},{16,8},{20,12},{24,16},{28,20},{1,25},{... | collective-permute-start | bytes 4718600 | tf_op jit(solution)/shard_map/ppermute | solution.py:9
  240.6 102.6 %collective-permute-start.4 = (bf16[2048,384]{1,0:T(8,128)(2,1)}, bf16[2048,384]{1,0:T(8,128)(2,1)}, u32[]{:S(2)}, u32[]{:S(2)}) collective-permute-start(bf16[2048,384]{1,0:T(8,128)(2,1)} %convert_element_type.147), channel_id=1, source_target_pairs={{0,8},{4,12},{8,16},{12,20},{16,24},{20,28},{24,0},{28,4},{1,9},{5... | collective-permute-start | bytes 4718600 | tf_op jit(solution)/shard_map/ppermute | solution.py:9
  266.6 82.7 %all-to-all-start.5 = ((bf16[16,128,384]{2,0,1:T(8,128)(2,1)}), bf16[16,128,384]{2,0,1:T(8,128)(2,1)}, u32[]{:S(2)}, u32[]{:S(2)}) async-start(bf16[16,128,384]{2,0,1:T(8,128)(2,1)} %copy.95), calls=%async_computation.5 | async-start | bytes 3145728 | tf_op jit(solution)/shard_map/all_to_all | solution.py:17
  274.0 69.2 %copy-start.17 = (bf16[1,16,128,128]{3,2,1,0:T(8,128)(2,1)S(1)}, bf16[1,16,128,128]{3,2,1,0:T(8,128)(2,1)}, u32[]{:S(2)}) copy-start(bf16[1,16,128,128]{3,2,1,0:T(8,128)(2,1)} %param.13) | copy-start | bytes 1572868
  349.2 24.9 %all-to-all-start.7 = ((bf16[16,128,384]{2,0,1:T(8,128)(2,1)}), bf16[16,128,384]{2,0,1:T(8,128)(2,1)}, u32[]{:S(2)}, u32[]{:S(2)}) async-start(bf16[16,128,384]{2,0,1:T(8,128)(2,1)} %copy.103), calls=%async_computation.7 | async-start | bytes 3145728 | tf_op jit(solution)/shard_map/all_to_all | solution.py:17
  374.1 24.7 %all-to-all-start.6 = ((bf16[64,32,384]{2,1,0:T(8,128)(2,1)}), bf16[64,32,384]{2,1,0:T(8,128)(2,1)}, u32[]{:S(2)}, u32[]{:S(2)}) async-start(bf16[64,32,384]{2,1,0:T(8,128)(2,1)} %copy.99), calls=%async_computation.6 | async-start | bytes 3145728 | tf_op jit(solution)/shard_map/all_to_all | solution.py:21
  380.5 12.2 %copy-start.26 = (bf16[4,16,32,384]{3,1,0,2:T(8,128)(2,1)}, bf16[4,16,32,384]{3,1,0,2:T(8,128)(2,1)S(1)}, u32[]{:S(2)}) copy-start(bf16[4,16,32,384]{3,1,0,2:T(8,128)(2,1)S(1)} %copy.105) | copy-start | bytes 4718596
  398.8 24.5 %all-to-all-start.9 = ((bf16[64,32,384]{2,1,0:T(8,128)(2,1)}), bf16[64,32,384]{2,1,0:T(8,128)(2,1)}, u32[]{:S(2)}, u32[]{:S(2)}) async-start(bf16[64,32,384]{2,1,0:T(8,128)(2,1)} %copy.110), calls=%async_computation.9 | async-start | bytes 3145728 | tf_op jit(solution)/shard_map/all_to_all | solution.py:21
  417.6 68.6 %collective-permute-start.6 = (bf16[2048,384]{1,0:T(8,128)(2,1)}, bf16[2048,384]{1,0:T(8,128)(2,1)S(1)}, u32[]{:S(2)}, u32[]{:S(2)}) collective-permute-start(bf16[2048,384]{1,0:T(8,128)(2,1)} %bitcast.222), channel_id=1, source_target_pairs={{0,4},{4,8},{8,12},{12,16},{16,20},{20,24},{24,28},{28,0},{1,5},{5... | collective-permute-start | bytes 4718600 | tf_op jit(solution)/shard_map/ppermute | solution.py:9
  425.1 11.5 %slice-start.2 = ((s8[6291456]{0:T(1024)(128)(4,1)}), s8[4194304]{0:T(1024)(128)(4,1)S(1)}, s32[]{:S(2)}) async-start(s8[6291456]{0:T(1024)(128)(4,1)} %bitcast.263), calls=%async_computation.14 | async-start | bytes 8388608
  426.9 65.8 %collective-permute-start.7 = (bf16[2048,384]{1,0:T(8,128)(2,1)}, bf16[2048,384]{1,0:T(8,128)(2,1)}, u32[]{:S(2)}, u32[]{:S(2)}) collective-permute-start(bf16[2048,384]{1,0:T(8,128)(2,1)} %bitcast.69), channel_id=1, source_target_pairs={{0,28},{4,0},{8,4},{12,8},{16,12},{20,16},{24,20},{28,24},{1,29},{... | collective-permute-start | bytes 4718600 | tf_op jit(solution)/shard_map/ppermute | solution.py:9
  439.2 51.4 %copy-start.8 = (bf16[1,1,2048,384]{3,2,1,0:T(8,128)(2,1)S(1)}, bf16[1,1,2048,384]{3,2,1,0:T(8,128)(2,1)}, u32[]{:S(2)}) copy-start(bf16[1,1,2048,384]{3,2,1,0:T(8,128)(2,1)} %copy-done.7) | copy-start | bytes 4718596
  439.2 51.4 %copy-start.24 = (f32[16,128,128]{2,1,0:T(8,128)S(1)}, f32[16,128,128]{2,1,0:T(8,128)}, u32[]{:S(2)}) copy-start(f32[16,128,128]{2,1,0:T(8,128)} %fusion.107) | copy-start | bytes 3145732
  (23 other events, 96.7 us)
where the time goes:
time: 508 us; the launch traced here: 498 us
  waiting for transfers between devices  228 us (45%)
  matrix products  116 us (23%)
  starting transfers between devices  65.9 us (13%)
  local copies, waits for them, and re-layouts  63.2 us (12%)
  other arithmetic  23 us (5%)
    ppermute x8, waiting for transfers between devices, shifted(): lax.ppermute(value, axis, [(i, (i + by) % count) for i in range(count)])  167 us
    all_to_all x6, waiting for transfers between devices, to_rows(): lax.all_to_all(value, 'tensor', split_axis=0, concat_axis=1, tiled=True)  34.6 us
    all_to_all x6, starting transfers between devices, to_columns(): lax.all_to_all(value, 'tensor', split_axis=1, concat_axis=0, tiled=True)  26.8 us
    all_to_all x6, waiting for transfers between devices, to_columns(): lax.all_to_all(value, 'tensor', split_axis=1, concat_axis=0, tiled=True)  26.5 us
    all_to_all x6, starting transfers between devices, to_rows(): lax.all_to_all(value, 'tensor', split_axis=0, concat_axis=1, tiled=True)  26.5 us
    dot_general x4, matrix products, front(): jnp.einsum('ifr,inf->nir', hidden, first_down, preferred_element_type=jnp...  25.2 us
    dot_general x2, matrix products, backward(): jnp.einsum('nir,inf->ifr', grad_folded, first_down, preferred_element_typ...  24.4 us
    dot_general x2, matrix products, backward(): jnp.einsum('ifr,nir->inf', hidden, grad_folded, preferred_element_type=jn...  15.3 us
  transfers between devices with their start and end apart: 20, of which 15 were waited for; matrix products, arithmetic and copies ran while one was open for 38% of the time, Pallas kernels for 0%

commit v1 on v0

--- a/solution.py
+++ b/solution.py
@@ -14,7 +14,12 @@
 
 
 def to_columns(value):
-    return lax.all_to_all(value, "tensor", split_axis=1, concat_axis=0, tiled=True)
+    return jnp.concatenate(
+        lax.all_to_all(
+            jnp.stack(jnp.split(value, lax.axis_size("tensor"), axis=1)), "tensor", 0, 0
+        ),
+        axis=0,
+    )
 
 
 def to_rows(value):

time: 508 us -> 466 us (0.917)
  waiting for transfers between devices: 228 us -> 191 us
  local copies, waits for them, and re-layouts: 63.2 us -> 37 us
  starting transfers between devices: 65.9 us -> 75.5 us
  matrix products: 116 us -> 123 us
  other arithmetic: 23 us -> 29.7 us
    ppermute x8, waiting for transfers between devices: 167 us -> 122 us  [shifted(): lax.ppermute(value, axis, [(i, (i + by) % count) for i in range(count)])]
    convert_element_type x6 -> x0, local copies, waits for them, and re-layouts: 14.9 us -> none  [the longest x4 9.09 us: front(): first_out = jnp.einsum('njr,nji->nir', narrow_in, first_up, preferred_ele...]
    all_to_all x6, waiting for transfers between devices: 26.5 us -> 40.1 us  [to_columns(): lax.all_to_all(jnp.stack(jnp.split(value, lax.axis_size('tensor'), axis=1...]
    all_to_all x6 -> x0, local copies, waits for them, and re-layouts: 12.6 us -> none  [to_columns(): lax.all_to_all(value, 'tensor', split_axis=1, concat_axis=0, tiled=True)]
    ppermute x8, starting transfers between devices: 12.6 us -> 23.8 us  [shifted(): lax.ppermute(value, axis, [(i, (i + by) % count) for i in range(count)])]
    another operation x0 -> x6, other arithmetic: none -> 9.44 us  [to_columns(): jnp.stack(jnp.split(value, lax.axis_size('tensor'), axis=1))]
    all_to_all x6, waiting for transfers between devices: 34.6 us -> 28.7 us  [to_rows(): lax.all_to_all(value, 'tensor', split_axis=0, concat_axis=1, tiled=True)]
where the time goes in v1:
time: 466 us; the launch traced here: 458 us
  waiting for transfers between devices  191 us (41%)
  matrix products  123 us (26%)
  starting transfers between devices  75.5 us (16%)
  local copies, waits for them, and re-layouts  37 us (8%)
  other arithmetic  29.7 us (6%)
    ppermute x8, waiting for transfers between devices, shifted(): lax.ppermute(value, axis, [(i, (i + by) % count) for i in range(count)])  122 us
    all_to_all x6, waiting for transfers between devices, to_columns(): lax.all_to_all(jnp.stack(jnp.split(value, lax.axis_size('tensor'), axis=1...  40.1 us
    all_to_all x6, waiting for transfers between devices, to_rows(): lax.all_to_all(value, 'tensor', split_axis=0, concat_axis=1, tiled=True)  28.7 us
    dot_general x2, matrix products, backward(): jnp.einsum('nir,inf->ifr', grad_folded, first_down, preferred_element_typ...  27.4 us
    all_to_all x6, starting transfers between devices, to_rows(): lax.all_to_all(value, 'tensor', split_axis=0, concat_axis=1, tiled=True)  26.1 us
    all_to_all x6, starting transfers between devices, to_columns(): lax.all_to_all(jnp.stack(jnp.split(value, lax.axis_size('tensor'), axis=1...  25.6 us
    dot_general x4, matrix products, front(): jnp.einsum('ifr,inf->nir', hidden, first_down, preferred_element_type=jnp...  25.4 us
    ppermute x8, starting transfers between devices, shifted(): lax.ppermute(value, axis, [(i, (i + by) % count) for i in range(count)])  23.8 us
  transfers between devices with their start and end apart: 20, of which 15 were waited for; matrix products, arithmetic and copies ran while one was open for 38% of the time, Pallas kernels for 0%

profile of v1, /device:TPU:0, one launch (start us, length us, event | category | flops | bytes accessed | tf_op | source)
XLA Modules:
  0.0 457.8 jit_solution(9751749375348364887)
XLA Ops:
  9.3 4.5 collective-permute-start.1
  13.7 15.6 %all-to-all-done = bf16[4,16,32,384]{3,2,1,0:T(8,128)(2,1)S(1)} async-done(((bf16[4,16,32,384]{3,2,1,0:T(8,128)(2,1)}), bf16[4,16,32,384]{3,2,1,0:T(8,128)(2,1)S(1)}, u32[]{:S(2)}, u32[]{:S(2)}) %all-to-all-start) | async-done | bytes 1572896 | tf_op jit(solution)/shard_map/all_to_all | solution.py:18
  29.4 7.4 %fusion.61 = bf16[64,32,384]{2,0,1:T(8,128)(2,1)} fusion(bf16[64,32,384]{2,1,0:T(8,128)(2,1)S(1)} %bitcast.307, bf16[1,32,64,256]{3,2,1,0:T(8,128)(2,1)} %param.12, bf16[1,32,64,256]{3,2,1,0:T(8,128)(2,1)S(1)} %copy-done), kind=kOutput, calls=%fused_computation.82 | convolution fusion | flops 834404352 | bytes 5242880 | tf_op jit(solution)/shard_map/ifr,inf->nir/dot_general | solution.py:36
  50.5 13.3 %all-to-all-done.1 = bf16[64,32,384]{2,1,0:T(8,128)(2,1)S(1)} async-done(((bf16[64,32,384]{2,1,0:T(8,128)(2,1)}), bf16[64,32,384]{2,1,0:T(8,128)(2,1)S(1)}, u32[]{:S(2)}, u32[]{:S(2)}) %all-to-all-start.1) | async-done | bytes 1572896 | tf_op jit(solution)/shard_map/all_to_all | solution.py:26
  77.7 10.9 %all-to-all-done.3 = bf16[4,16,32,384]{3,2,1,0:T(8,128)(2,1)S(1)} async-done(((bf16[4,16,32,384]{3,2,1,0:T(8,128)(2,1)}), bf16[4,16,32,384]{3,2,1,0:T(8,128)(2,1)S(1)}, u32[]{:S(2)}, u32[]{:S(2)}) %all-to-all-start.3) | async-done | bytes 1572896 | tf_op jit(solution)/shard_map/all_to_all | solution.py:18
  88.6 4.6 %all-to-all-start.2 = ((bf16[4,16,32,384]{3,2,1,0:T(8,128)(2,1)}), bf16[4,16,32,384]{3,2,1,0:T(8,128)(2,1)}, u32[]{:S(2)}, u32[]{:S(2)}) async-start(bf16[4,16,32,384]{3,2,1,0:T(8,128)(2,1)} %pad_maximum_fusion.1), calls=%async_computation.2 | async-start | bytes 3145728 | tf_op jit(solution)/shard_map/all_to_all | solution.py:18
  95.7 8.8 %fusion.34 = (bf16[32,256,384]{1,2,0:T(8,128)(2,1)}, f32[32,384,256]{2,1,0:T(8,128)}) fusion(bf16[1,32,64,256]{3,2,1,0:T(8,128)(2,1)S(1)} %copy-done, bf16[64,32,384]{2,1,0:T(8,128)(2,1)S(1)} %bitcast.299), kind=kOutput, calls=%fused_computation.45 | convolution fusion | flops 430964736 | bytes 21495808 | tf_op jit(solution)/shard_map/nir,inf->ifr/dot_general | solution.py:34
  104.5 8.8 %all-to-all-done.2 = bf16[4,16,32,384]{3,2,1,0:T(8,128)(2,1)} async-done(((bf16[4,16,32,384]{3,2,1,0:T(8,128)(2,1)}), bf16[4,16,32,384]{3,2,1,0:T(8,128)(2,1)}, u32[]{:S(2)}, u32[]{:S(2)}) %all-to-all-start.2) | async-done | bytes 1572896 | tf_op jit(solution)/shard_map/all_to_all | solution.py:18
  113.3 4.4 all-to-all-start.8
  117.7 13.6 %fusion.6 = bf16[32,256,384]{1,2,0:T(8,128)(2,1)S(1)} fusion(f32[32,384,256]{2,1,0:T(8,128)} %get-tuple-element.63, bf16[64,32,384]{2,1,0:T(8,128)(2,1)} %bitcast.24, bf16[1,32,64,256]{3,2,1,0:T(8,128)(2,1)S(1)} %copy-done.27), kind=kOutput, calls=%fused_computation.12 | convolution fusion | flops 465567744 | bytes 21495808 | tf_op jit(solution)/shard_map/nir,inf->ifr/dot_general | solution.py:56
  137.8 4.9 %all-to-all-start.4 = ((bf16[64,32,384]{2,1,0:T(8,128)(2,1)}), bf16[64,32,384]{2,1,0:T(8,128)(2,1)}, u32[]{:S(2)}, u32[]{:S(2)}) async-start(bf16[64,32,384]{2,1,0:T(8,128)(2,1)} %copy.56), calls=%async_computation.4 | async-start | bytes 3145728 | tf_op jit(solution)/shard_map/all_to_all | solution.py:26
  142.8 8.0 %fusion.74 = f32[32,384,256]{2,1,0:T(8,128)} fusion(bf16[64,32,384]{2,1,0:T(8,128)(2,1)} %bitcast.71, bf16[1,32,64,256]{3,2,1,0:T(8,128)(2,1)S(1)} %copy-done), kind=kOutput, calls=%fused_computation.91 | convolution fusion | flops 402653184 | bytes 15204352 | tf_op jit(solution)/shard_map/nir,inf->ifr/dot_general | solution.py:34
  162.9 4.3 all-to-all-start.10
  167.2 7.9 %fusion.69 = bf16[64,32,384]{2,0,1:T(8,128)(2,1)S(1)} fusion(bf16[1,32,64,256]{3,2,1,0:T(8,128)(2,1)S(1)} %copy-done.29, f32[32,384,256]{2,1,0:T(8,128)} %fusion.74), kind=kOutput, calls=%fused_computation.86 | convolution fusion | flops 431751168 | bytes 15204352 | tf_op jit(solution)/shard_map/ifr,inf->nir/dot_general | solution.py:36
  181.3 6.1 %all-to-all-done.10 = bf16[64,32,384]{2,1,0:T(8,128)(2,1)} async-done(((bf16[64,32,384]{2,1,0:T(8,128)(2,1)}), bf16[64,32,384]{2,1,0:T(8,128)(2,1)}, u32[]{:S(2)}, u32[]{:S(2)}) %all-to-all-start.10) | async-done | bytes 1572896 | tf_op jit(solution)/shard_map/all_to_all | solution.py:26
  191.7 4.4 add_convert_fusion
  211.8 4.5 all-to-all-start.5
  222.8 14.7 %collective-permute-done.4 = bf16[2048,384]{1,0:T(8,128)(2,1)} collective-permute-done((bf16[2048,384]{1,0:T(8,128)(2,1)}, bf16[2048,384]{1,0:T(8,128)(2,1)}, u32[]{:S(2)}, u32[]{:S(2)}) %collective-permute-start.4) | collective-permute-done | bytes 1572896 | tf_op jit(solution)/shard_map/ppermute | solution.py:9
  237.5 33.5 %collective-permute-done.5 = bf16[2048,384]{1,0:T(8,128)(2,1)} collective-permute-done((bf16[2048,384]{1,0:T(8,128)(2,1)}, bf16[2048,384]{1,0:T(8,128)(2,1)}, u32[]{:S(2)}, u32[]{:S(2)}) %collective-permute-start.5) | collective-permute-done | bytes 1572896 | tf_op jit(solution)/shard_map/ppermute | solution.py:9
  271.0 30.9 %collective-permute-done.3 = bf16[2048,384]{1,0:T(8,128)(2,1)} collective-permute-done((bf16[2048,384]{1,0:T(8,128)(2,1)}, bf16[2048,384]{1,0:T(8,128)(2,1)}, u32[]{:S(2)}, u32[]{:S(2)}) %collective-permute-start.3) | collective-permute-done | bytes 1572896 | tf_op jit(solution)/shard_map/ppermute | solution.py:9
  305.5 4.3 all-to-all-start.7
  309.8 5.8 %fusion.82 = f32[32,64,256]{2,1,0:T(8,128)} fusion(bf16[32,256,384]{1,2,0:T(8,128)(2,1)} %get-tuple-element.62, bf16[64,32,384]{2,1,0:T(8,128)(2,1)} %bitcast.24), kind=kOutput, calls=%fused_computation.99 | convolution fusion | flops 402653184 | bytes 9961472 | tf_op jit(solution)/shard_map/ifr,nir->inf/dot_general | solution.py:53
  315.6 8.0 %fusion.56 = bf16[64,32,384]{2,0,1:T(8,128)(2,1)} fusion(bf16[64,32,384]{2,1,0:T(8,128)(2,1)} %bitcast.47, bf16[1,32,64,256]{3,2,1,0:T(8,128)(2,1)} %param.12, bf16[1,32,64,256]{3,2,1,0:T(8,128)(2,1)S(1)} %copy-done), kind=kOutput, calls=%fused_computation.81 | convolution fusion | flops 834404352 | bytes 5242880 | tf_op jit(solution)/shard_map/ifr,inf->nir/dot_general | solution.py:36
  330.0 4.6 %all-to-all-start.6 = ((bf16[64,32,384]{2,1,0:T(8,128)(2,1)}), bf16[64,32,384]{2,1,0:T(8,128)(2,1)}, u32[]{:S(2)}, u32[]{:S(2)}) async-start(bf16[64,32,384]{2,1,0:T(8,128)(2,1)} %copy.61), calls=%async_computation.6 | async-start | bytes 3145728 | tf_op jit(solution)/shard_map/all_to_all | solution.py:26
  334.5 13.8 %fusion.13 = bf16[32,256,384]{1,2,0:T(8,128)(2,1)S(1)} fusion(f32[32,384,256]{2,1,0:T(8,128)} %fusion.74, bf16[64,32,384]{2,1,0:T(8,128)(2,1)} %bitcast.64, bf16[1,32,64,256]{3,2,1,0:T(8,128)(2,1)} %param.12), kind=kOutput, calls=%fused_computation.19 | convolution fusion | flops 465567744 | bytes 21495808 | tf_op jit(solution)/shard_map/nir,inf->ifr/dot_general | solution.py:56
  354.7 4.3 all-to-all-start.9
  359.0 5.9 %fusion.78 = f32[32,64,256]{2,1,0:T(8,128)} fusion(bf16[32,256,384]{1,2,0:T(8,128)(2,1)} %copy-done.4, bf16[64,32,384]{2,1,0:T(8,128)(2,1)} %bitcast.300), kind=kOutput, calls=%fused_computation.95 | convolution fusion | flops 402653184 | bytes 9961472 | tf_op jit(solution)/shard_map/nir,ifr->inf/dot_general | solution.py:61
  382.7 5.5 %collective-permute-start.7 = (bf16[2048,384]{1,0:T(8,128)(2,1)}, bf16[2048,384]{1,0:T(8,128)(2,1)}, u32[]{:S(2)}, u32[]{:S(2)}) collective-permute-start(bf16[2048,384]{1,0:T(8,128)(2,1)} %bitcast.78), channel_id=1, source_target_pairs={{0,28},{4,0},{8,4},{12,8},{16,12},{20,16},{24,20},{28,24},{1,29},{... | collective-permute-start | bytes 4718600 | tf_op jit(solution)/shard_map/ppermute | solution.py:9
  388.3 10.8 %add_bitcast_fusion.2 = f32[1,32,64,256]{3,2,1,0:T(8,128)} fusion(f32[32,64,256]{2,1,0:T(8,128)S(1)} %copy-done.26, bf16[64,32,384]{2,1,0:T(8,128)(2,1)} %bitcast.64, f32[32,384,256]{2,1,0:T(8,128)} %fusion.74), kind=kOutput, calls=%fused_computation.58 | convolution fusion | flops 431489024 | bytes 18350080 | tf_op jit(solution)/shard_map/ifr,nir->inf/dot_general | solution.py:53
  403.1 42.8 %collective-permute-done.6 = bf16[2048,384]{1,0:T(8,128)(2,1)S(1)} collective-permute-done((bf16[2048,384]{1,0:T(8,128)(2,1)}, bf16[2048,384]{1,0:T(8,128)(2,1)S(1)}, u32[]{:S(2)}, u32[]{:S(2)}) %collective-permute-start.6) | collective-permute-done | bytes 1572896 | tf_op jit(solution)/shard_map/ppermute | solution.py:9
  445.9 4.4 add_bitcast_fusion.1
  452.5 4.9 %add_bitcast_fusion = f32[1,2048,384]{2,1,0:T(8,128)} fusion(f32[2048,384]{1,0:T(8,128)} %collective-permute-done.1, bf16[2048,384]{1,0:T(8,128)(2,1)} %collective-permute-done.7, bf16[2048,384]{1,0:T(8,128)(2,1)} %collective-permute-done.5), kind=kLoop, calls=%fused_computation.54 | loop fusion | flops 3145728 | bytes 9437184 | tf_op jit(solution)/shard_map/broadcast_in_dim | solution.py:136
  (140 shorter events, 129.9 us)
Async XLA Ops:
  0.6 28.7 %copy-start = (bf16[1,32,64,256]{3,2,1,0:T(8,128)(2,1)S(1)}, bf16[1,32,64,256]{3,2,1,0:T(8,128)(2,1)}, u32[]{:S(2)}) copy-start(bf16[1,32,64,256]{3,2,1,0:T(8,128)(2,1)} %param.11) | copy-start | bytes 3145732
  5.1 24.3 %all-to-all-start = ((bf16[4,16,32,384]{3,2,1,0:T(8,128)(2,1)}), bf16[4,16,32,384]{3,2,1,0:T(8,128)(2,1)S(1)}, u32[]{:S(2)}, u32[]{:S(2)}) async-start(bf16[4,16,32,384]{3,2,1,0:T(8,128)(2,1)} %pad_maximum_fusion), calls=%async_computation | async-start | bytes 3145728 | tf_op jit(solution)/shard_map/all_to_all | solution.py:18
  9.3 186.9 %collective-permute-start.1 = (f32[2048,384]{1,0:T(8,128)}, f32[2048,384]{1,0:T(8,128)}, u32[]{:S(2)}, u32[]{:S(2)}) collective-permute-start(f32[2048,384]{1,0:T(8,128)} %bitcast.295), channel_id=1, source_target_pairs={{0,24},{4,28},{8,0},{12,4},{16,8},{20,12},{24,16},{28,20},{1,25},{... | collective-permute-start | bytes 9437192 | tf_op jit(solution)/shard_map/ppermute | solution.py:9
  13.7 182.4 %collective-permute-start = (f32[2048,384]{1,0:T(8,128)}, f32[2048,384]{1,0:T(8,128)}, u32[]{:S(2)}, u32[]{:S(2)}) collective-permute-start(f32[2048,384]{1,0:T(8,128)} %bitcast.298), channel_id=1, source_target_pairs={{0,8},{4,12},{8,16},{12,20},{16,24},{20,28},{24,0},{28,4},{1,9},{5... | collective-permute-start | bytes 9437192 | tf_op jit(solution)/shard_map/ppermute | solution.py:9
  40.2 23.6 %all-to-all-start.1 = ((bf16[64,32,384]{2,1,0:T(8,128)(2,1)}), bf16[64,32,384]{2,1,0:T(8,128)(2,1)S(1)}, u32[]{:S(2)}, u32[]{:S(2)}) async-start(bf16[64,32,384]{2,1,0:T(8,128)(2,1)} %copy.49), calls=%async_computation.1 | async-start | bytes 3145728 | tf_op jit(solution)/shard_map/all_to_all | solution.py:26
  65.0 23.6 %all-to-all-start.3 = ((bf16[4,16,32,384]{3,2,1,0:T(8,128)(2,1)}), bf16[4,16,32,384]{3,2,1,0:T(8,128)(2,1)S(1)}, u32[]{:S(2)}, u32[]{:S(2)}) async-start(bf16[4,16,32,384]{3,2,1,0:T(8,128)(2,1)} %pad_maximum_fusion.2), calls=%async_computation.3 | async-start | bytes 3145728 | tf_op jit(solution)/shard_map/all_to_all | solution.py:18
  88.6 24.7 %all-to-all-start.2 = ((bf16[4,16,32,384]{3,2,1,0:T(8,128)(2,1)}), bf16[4,16,32,384]{3,2,1,0:T(8,128)(2,1)}, u32[]{:S(2)}, u32[]{:S(2)}) async-start(bf16[4,16,32,384]{3,2,1,0:T(8,128)(2,1)} %pad_maximum_fusion.1), calls=%async_computation.2 | async-start | bytes 3145728 | tf_op jit(solution)/shard_map/all_to_all | solution.py:18
  104.5 13.2 %copy-start.27 = (bf16[1,32,64,256]{3,2,1,0:T(8,128)(2,1)S(1)}, bf16[1,32,64,256]{3,2,1,0:T(8,128)(2,1)}, u32[]{:S(2)}) copy-start(bf16[1,32,64,256]{3,2,1,0:T(8,128)(2,1)} %param.12) | copy-start | bytes 3145732
  113.3 24.5 %all-to-all-start.8 = ((bf16[4,16,32,384]{3,2,1,0:T(8,128)(2,1)}), bf16[4,16,32,384]{3,2,1,0:T(8,128)(2,1)}, u32[]{:S(2)}, u32[]{:S(2)}) async-start(bf16[4,16,32,384]{3,2,1,0:T(8,128)(2,1)} %pad_maximum_fusion.5), calls=%async_computation.8 | async-start | bytes 3145728 | tf_op jit(solution)/shard_map/all_to_all | solution.py:18
  137.8 12.9 %slice-start = ((s8[6291456]{0:T(1024)(128)(4,1)}), s8[2097152]{0:T(1024)(128)(4,1)S(1)}, s32[]{:S(2)}) async-start(s8[6291456]{0:T(1024)(128)(4,1)} %bitcast.281), calls=%async_computation.12 | async-start | bytes 4194304
  137.8 25.0 %all-to-all-start.4 = ((bf16[64,32,384]{2,1,0:T(8,128)(2,1)}), bf16[64,32,384]{2,1,0:T(8,128)(2,1)}, u32[]{:S(2)}, u32[]{:S(2)}) async-start(bf16[64,32,384]{2,1,0:T(8,128)(2,1)} %copy.56), calls=%async_computation.4 | async-start | bytes 3145728 | tf_op jit(solution)/shard_map/all_to_all | solution.py:26
  142.7 8.0 %slice-start.1 = ((s8[6291456]{0:T(1024)(128)(4,1)}), s8[4194304]{0:T(1024)(128)(4,1)S(1)}, s32[]{:S(2)}) async-start(s8[6291456]{0:T(1024)(128)(4,1)} %bitcast.281), calls=%async_computation.13 | async-start | bytes 8388608
  156.4 10.8 %copy-start.29 = (bf16[1,32,64,256]{3,2,1,0:T(8,128)(2,1)S(1)}, bf16[1,32,64,256]{3,2,1,0:T(8,128)(2,1)}, u32[]{:S(2)}) copy-start(bf16[1,32,64,256]{3,2,1,0:T(8,128)(2,1)} %param.12) | copy-start | bytes 3145732
  156.4 49.7 %collective-permute-start.2 = (bf16[2048,384]{1,0:T(8,128)(2,1)}, bf16[2048,384]{1,0:T(8,128)(2,1)}, u32[]{:S(2)}, u32[]{:S(2)}) collective-permute-start(bf16[2048,384]{1,0:T(8,128)(2,1)} %add_convert_fusion.1), channel_id=1, source_target_pairs={{0,4},{4,8},{8,12},{12,16},{16,20},{20,24},{24,28},{28,0},{1,5},{5... | collective-permute-start | bytes 4718600 | tf_op jit(solution)/shard_map/ppermute | solution.py:9
  162.9 24.5 %all-to-all-start.10 = ((bf16[64,32,384]{2,1,0:T(8,128)(2,1)}), bf16[64,32,384]{2,1,0:T(8,128)(2,1)}, u32[]{:S(2)}, u32[]{:S(2)}) async-start(bf16[64,32,384]{2,1,0:T(8,128)(2,1)} %copy.79), calls=%async_computation.10 | async-start | bytes 3145728 | tf_op jit(solution)/shard_map/all_to_all | solution.py:26
  187.4 24.5 %all-to-all-start.11 = ((bf16[64,32,384]{2,1,0:T(8,128)(2,1)}), bf16[64,32,384]{2,1,0:T(8,128)(2,1)}, u32[]{:S(2)}, u32[]{:S(2)}) async-start(bf16[64,32,384]{2,1,0:T(8,128)(2,1)} %copy.82), calls=%async_computation.11 | async-start | bytes 3145728 | tf_op jit(solution)/shard_map/all_to_all | solution.py:26
  197.5 40.0 %collective-permute-start.4 = (bf16[2048,384]{1,0:T(8,128)(2,1)}, bf16[2048,384]{1,0:T(8,128)(2,1)}, u32[]{:S(2)}, u32[]{:S(2)}) collective-permute-start(bf16[2048,384]{1,0:T(8,128)(2,1)} %convert_element_type.147), channel_id=1, source_target_pairs={{0,8},{4,12},{8,16},{12,20},{16,24},{20,28},{24,0},{28,4},{1,9},{5... | collective-permute-start | bytes 4718600 | tf_op jit(solution)/shard_map/ppermute | solution.py:9
  201.2 69.8 %collective-permute-start.5 = (bf16[2048,384]{1,0:T(8,128)(2,1)}, bf16[2048,384]{1,0:T(8,128)(2,1)}, u32[]{:S(2)}, u32[]{:S(2)}) collective-permute-start(bf16[2048,384]{1,0:T(8,128)(2,1)} %convert_element_type.148), channel_id=1, source_target_pairs={{0,24},{4,28},{8,0},{12,4},{16,8},{20,12},{24,16},{28,20},{1,25},{... | collective-permute-start | bytes 4718600 | tf_op jit(solution)/shard_map/ppermute | solution.py:9
  204.3 97.6 %collective-permute-start.3 = (bf16[2048,384]{1,0:T(8,128)(2,1)}, bf16[2048,384]{1,0:T(8,128)(2,1)}, u32[]{:S(2)}, u32[]{:S(2)}) collective-permute-start(bf16[2048,384]{1,0:T(8,128)(2,1)} %add_convert_fusion), channel_id=1, source_target_pairs={{0,28},{4,0},{8,4},{12,8},{16,12},{20,16},{24,20},{28,24},{1,29},{... | collective-permute-start | bytes 4718600 | tf_op jit(solution)/shard_map/ppermute | solution.py:9
  211.8 93.6 %all-to-all-start.5 = ((bf16[4,16,32,384]{3,2,1,0:T(8,128)(2,1)}), bf16[4,16,32,384]{3,2,1,0:T(8,128)(2,1)}, u32[]{:S(2)}, u32[]{:S(2)}) async-start(bf16[4,16,32,384]{3,2,1,0:T(8,128)(2,1)} %pad_maximum_fusion.3), calls=%async_computation.5 | async-start | bytes 3145728 | tf_op jit(solution)/shard_map/all_to_all | solution.py:18
  221.0 80.8 %copy-start.17 = (bf16[1,16,128,128]{3,2,1,0:T(8,128)(2,1)S(1)}, bf16[1,16,128,128]{3,2,1,0:T(8,128)(2,1)}, u32[]{:S(2)}) copy-start(bf16[1,16,128,128]{3,2,1,0:T(8,128)(2,1)} %param.13) | copy-start | bytes 1572868
  305.5 24.5 %all-to-all-start.7 = ((bf16[4,16,32,384]{3,2,1,0:T(8,128)(2,1)}), bf16[4,16,32,384]{3,2,1,0:T(8,128)(2,1)}, u32[]{:S(2)}, u32[]{:S(2)}) async-start(bf16[4,16,32,384]{3,2,1,0:T(8,128)(2,1)} %pad_maximum_fusion.4), calls=%async_computation.7 | async-start | bytes 3145728 | tf_op jit(solution)/shard_map/all_to_all | solution.py:18
  330.0 24.7 %all-to-all-start.6 = ((bf16[64,32,384]{2,1,0:T(8,128)(2,1)}), bf16[64,32,384]{2,1,0:T(8,128)(2,1)}, u32[]{:S(2)}, u32[]{:S(2)}) async-start(bf16[64,32,384]{2,1,0:T(8,128)(2,1)} %copy.61), calls=%async_computation.6 | async-start | bytes 3145728 | tf_op jit(solution)/shard_map/all_to_all | solution.py:26
  354.7 24.5 %all-to-all-start.9 = ((bf16[64,32,384]{2,1,0:T(8,128)(2,1)}), bf16[64,32,384]{2,1,0:T(8,128)(2,1)}, u32[]{:S(2)}, u32[]{:S(2)}) async-start(bf16[64,32,384]{2,1,0:T(8,128)(2,1)} %copy.68), calls=%async_computation.9 | async-start | bytes 3145728 | tf_op jit(solution)/shard_map/all_to_all | solution.py:26
  373.4 72.5 %collective-permute-start.6 = (bf16[2048,384]{1,0:T(8,128)(2,1)}, bf16[2048,384]{1,0:T(8,128)(2,1)S(1)}, u32[]{:S(2)}, u32[]{:S(2)}) collective-permute-start(bf16[2048,384]{1,0:T(8,128)(2,1)} %bitcast.252), channel_id=1, source_target_pairs={{0,4},{4,8},{8,12},{12,16},{16,20},{20,24},{24,28},{28,0},{1,5},{5... | collective-permute-start | bytes 4718600 | tf_op jit(solution)/shard_map/ppermute | solution.py:9
  379.2 9.1 %copy-start.26 = (f32[32,64,256]{2,1,0:T(8,128)S(1)}, f32[32,64,256]{2,1,0:T(8,128)}, u32[]{:S(2)}) copy-start(f32[32,64,256]{2,1,0:T(8,128)} %fusion.82) | copy-start | bytes 6291460
  381.0 18.1 %slice-start.2 = ((s8[6291456]{0:T(1024)(128)(4,1)}), s8[4194304]{0:T(1024)(128)(4,1)S(1)}, s32[]{:S(2)}) async-start(s8[6291456]{0:T(1024)(128)(4,1)} %bitcast.283), calls=%async_computation.14 | async-start | bytes 8388608
  382.7 16.3 %slice-start.3 = ((s8[6291456]{0:T(1024)(128)(4,1)}), s8[2097152]{0:T(1024)(128)(4,1)S(1)}, s32[]{:S(2)}) async-start(s8[6291456]{0:T(1024)(128)(4,1)} %bitcast.283), calls=%async_computation.15 | async-start | bytes 4194304
  382.7 16.3 %copy-start.19 = (f32[32,64,256]{2,1,0:T(8,128)S(1)}, f32[32,64,256]{2,1,0:T(8,128)}, u32[]{:S(2)}) copy-start(f32[32,64,256]{2,1,0:T(8,128)} %fusion.78) | copy-start | bytes 6291460
  382.7 69.7 %collective-permute-start.7 = (bf16[2048,384]{1,0:T(8,128)(2,1)}, bf16[2048,384]{1,0:T(8,128)(2,1)}, u32[]{:S(2)}, u32[]{:S(2)}) collective-permute-start(bf16[2048,384]{1,0:T(8,128)(2,1)} %bitcast.78), channel_id=1, source_target_pairs={{0,28},{4,0},{8,4},{12,8},{16,12},{20,16},{24,20},{28,24},{1,29},{... | collective-permute-start | bytes 4718600 | tf_op jit(solution)/shard_map/ppermute | solution.py:9
  403.1 47.2 %copy-start.9 = (bf16[1,1,2048,384]{3,2,1,0:T(8,128)(2,1)S(1)}, bf16[1,1,2048,384]{3,2,1,0:T(8,128)(2,1)}, u32[]{:S(2)}) copy-start(bf16[1,1,2048,384]{3,2,1,0:T(8,128)(2,1)} %copy-done.8) | copy-start | bytes 4718596
  403.1 47.2 %copy-start.25 = (f32[16,128,128]{2,1,0:T(8,128)S(1)}, f32[16,128,128]{2,1,0:T(8,128)}, u32[]{:S(2)}) copy-start(f32[16,128,128]{2,1,0:T(8,128)} %fusion.125) | copy-start | bytes 3145732
  (22 other events, 65.5 us)
